TPU v7x, 512 devices: a whole 4x8x8 slice. The times are simulated.
512 devices in a mesh: dom: 64 (over z_hi, y, core), cls: 8 (over z_lo, x).
Axes of the slice: x: 4, y: 8, z: 8 (z_hi: 4, z_lo: 2; z = z_hi * 2 + z_lo), core: 2. Of those that a mesh axis runs over, the one named last changes fastest.
Arguments:
- particles: bfloat16 [512, 64, 64], P(('dom', 'cls')), as said below
- group_ids: int32 [512], P(('dom', 'cls')), may hold values from 0 to 15
- references: float32 [96, 4096], P('cls', 'dom'), as said below
- ctf_profile: float32 [16, 23], replicated, may hold values from 0.1 to 1
- noise_power: float32 [23], replicated, may hold values from 2 to 16
Outputs:
- new_refs: float32 [2, 96, 1024], P(None, 'cls', 'dom')
- log_evidence: float32 [512], P('dom')
Inputs may be any that keep to these rules, and one draw needn't show every extreme that they name: `particles`: pixel values. `references`: pixel values.
All inputs are finite; a program needn't handle non-finite values.
Results may differ from a plain program's by a relative error of at most 0.011.
Values may be sent and summed in bfloat16 or wider, within the bound.
No kernel may reach another device: no remote copies, remote signals or barrier semaphores. Data moves between devices by JAX's collectives and lax.ppermute only.
A program may use at most 64 MiB of HBM per device.

v0:
```python
import math
import jax
import jax.numpy as jnp
from jax import lax
from jax.sharding import PartitionSpec as P

L = 64
BAND = 32
ROT = 8
NRAD = 23
GROUPS = 16
HIGHEST = lax.Precision.HIGHEST


def phase_tables(size, band):
    pixel = jnp.arange(size, dtype=jnp.int32)
    freq = jnp.arange(band, dtype=jnp.int32) - band // 2
    turned = freq[:, None] * pixel[None, :] % size
    angle = turned.astype(jnp.float32) * (2.0 * math.pi / size)
    return (jnp.cos(angle), jnp.sin(angle))


def forward_tables(cosine, sine):
    fcos = cosine / 8.0
    fsin = sine / 8.0
    first_table_part = jnp.stack([fcos.T, -fsin.T], axis=1)
    second_table_part = jnp.stack(
        [jnp.stack([fcos.T, -fsin.T], axis=1), jnp.stack([fsin.T, fcos.T], axis=1)], axis=1
    )
    return (first_table_part, second_table_part)


def inverse_tables(cosine, sine):
    icos = cosine.astype(jnp.bfloat16)
    isin = sine.astype(jnp.bfloat16)
    tab_c = jnp.stack([jnp.stack([icos, isin], axis=1), jnp.stack([-isin, icos], axis=1)], axis=0)
    tab_d = jnp.stack([icos, -isin], axis=0)
    tab_e = jnp.stack([icos.T, isin.T], axis=1)
    tab_f = jnp.stack(
        [jnp.stack([icos.T, isin.T], axis=1), jnp.stack([-isin.T, icos.T], axis=1)], axis=1
    )
    return (tab_c, tab_d, tab_e, tab_f)


def product(form, left, right):
    return jnp.einsum(form, left, right, preferred_element_type=jnp.float32)


def orient(images):
    turned = jnp.swapaxes(images, 1, 2)
    views = [jnp.rot90(images, j, axes=(1, 2)) for j in range(4)]
    views = views + [jnp.rot90(turned, j, axes=(1, 2)) for j in range(4)]
    return jnp.stack(views, axis=1)


def particle_band_rows(images, first_table_part, second_table_part):
    count = images.shape[0]
    oriented = orient(images)
    half = product("nryx,xdb->nrydb", oriented, first_table_part).astype(jnp.bfloat16)
    full = product("nrydb,ydca->nrcab", half, second_table_part).astype(jnp.bfloat16)
    return full.reshape(count, ROT, 2, BAND * BAND)


def class_bands(maps, first_table_part, second_table_part):
    count = maps.shape[0]
    images = maps.reshape(count, L, L)
    half = jnp.einsum("kyx,xdb->kydb", images, first_table_part, precision=HIGHEST)
    full = jnp.einsum("kydb,ydca->kcab", half, second_table_part, precision=HIGHEST)
    return full.reshape(count, 2, BAND * BAND)


def shell_onehot():
    freq = jnp.arange(BAND, dtype=jnp.int32) - BAND // 2
    square = (freq[:, None] ** 2 + freq[None, :] ** 2).reshape(-1)
    bounds = jnp.arange(1, NRAD, dtype=jnp.int32) ** 2
    shell = jnp.sum((square[None, :] >= bounds[:, None]).astype(jnp.int32), axis=0)
    return (shell[None, :] == jnp.arange(NRAD, dtype=jnp.int32)[:, None]).astype(jnp.float32)


def group_onehot(group_ids):
    return (group_ids[:, None] == jnp.arange(GROUPS, dtype=jnp.int32)[None, :]).astype(jnp.float32)


def spectra(ctf_profile, noise_power, group_ids):
    shells = shell_onehot()
    groups = group_onehot(group_ids)
    profile = jnp.dot(groups, ctf_profile, precision=HIGHEST)
    contrast_transfer = jnp.dot(profile, shells, precision=HIGHEST)
    noise_deviation = jnp.dot(noise_power, shells, precision=HIGHEST)
    return (contrast_transfer, noise_deviation)


def class_step(abstract_value, output_value, ref_band, offset, tabs):
    tab_c, tab_d, tab_e, tab_f = tabs
    count = abstract_value.shape[0]
    real_ref = ref_band[0]
    imag_ref = ref_band[1]
    breal = abstract_value[:, :, 0] * real_ref + abstract_value[:, :, 1] * imag_ref
    bimag = abstract_value[:, :, 1] * real_ref - abstract_value[:, :, 0] * imag_ref
    bmat = jnp.stack([breal, bimag], axis=2).astype(jnp.bfloat16).reshape(count, ROT, 2, BAND, BAND)
    edge = product("nrcab,cbdx->nradx", bmat, tab_c).astype(jnp.bfloat16)
    score = product("nradx,day->nyrx", edge, tab_d) - offset[:, None, None, None]
    peak = jnp.max(score, axis=(1, 2, 3))
    expo = jnp.exp(score - peak[:, None, None, None])
    total = jnp.sum(expo, axis=(1, 2, 3))
    uhalf = product("nyrx,xdb->nrydb", expo.astype(jnp.bfloat16), tab_e).astype(jnp.bfloat16)
    what = product("nrydb,ydca->nrcab", uhalf, tab_f).astype(jnp.bfloat16)
    what = what.reshape(count, ROT, 2, BAND * BAND).astype(jnp.float32)
    preal = jnp.sum(
        output_value[:, :, 0] * what[:, :, 0] - output_value[:, :, 1] * what[:, :, 1], axis=1
    )
    pimag = jnp.sum(
        output_value[:, :, 0] * what[:, :, 1] + output_value[:, :, 1] * what[:, :, 0], axis=1
    )
    return (peak, total, jnp.stack([preal, pimag], axis=1))


def shards(particles, group_ids, references, ctf_profile, noise_power):
    cosine, sine = phase_tables(L, BAND)
    first_table_part, second_table_part = forward_tables(cosine, sine)
    tabs = inverse_tables(cosine, sine)
    first_low = first_table_part.astype(jnp.bfloat16)
    second_low = second_table_part.astype(jnp.bfloat16)
    own_bands = particle_band_rows(particles, first_low, second_low)
    fourier_input, block_labels = (
        lax.all_gather(own_bands, "cls", axis=0, tiled=True),
        lax.all_gather(group_ids, "cls", axis=0, tiled=True),
    )
    maps = lax.all_gather(references, "dom", axis=1, tiled=True)
    complete_input = fourier_input.astype(jnp.float32)
    contrast_transfer, noise_deviation = spectra(ctf_profile, noise_power, block_labels)
    abstract_value = (
        complete_input * (contrast_transfer / noise_deviation[None, :])[:, None, None, :]
    )
    output_value = complete_input * contrast_transfer[:, None, None, :]
    rbands = class_bands(maps, first_table_part, second_table_part)
    power = rbands[:, 0] ** 2 + rbands[:, 1] ** 2
    offset = 0.5 * jnp.dot(
        contrast_transfer * contrast_transfer / noise_deviation[None, :], power.T, precision=HIGHEST
    )
    peaks, totals, projs = lax.map(
        lambda item: class_step(abstract_value, output_value, item[0], item[1], tabs),
        (rbands, offset.T),
    )
    local_top = jnp.max(peaks, axis=0)
    top = lax.pmax(local_top, "cls")
    mass = lax.psum(jnp.sum(jnp.exp(peaks - top[None, :]) * totals, axis=0), "cls")
    log_evidence = top + jnp.log(mass)
    share = jnp.exp(peaks - top[None, :]) / mass[None, :]
    numer = jnp.einsum("kp,kpcf->ckf", share, projs, precision=HIGHEST)
    denom = jnp.dot(share * totals, contrast_transfer * contrast_transfer, precision=HIGHEST)
    stacked = jnp.concatenate([numer, denom[None]], axis=0)
    owned = lax.psum_scatter(stacked, "dom", scatter_dimension=2, tiled=True)
    new_refs = owned[:2] / (owned[2] + 1.0)[None]
    return (new_refs, log_evidence)


def solution(mesh):
    in_specs = (P(("dom", "cls"), None, None), P(("dom", "cls")), P("cls", "dom"), P(), P())
    out_specs = (P(None, "cls", "dom"), P("dom"))
    return jax.shard_map(shards, mesh=mesh, in_specs=in_specs, out_specs=out_specs, check_vma=False)
```

profile of v0, /device:TPU:4, one launch (start us, length us, event | category | flops | bytes accessed | tf_op | source)
XLA Modules:
  0.0 478.3 jit_solution(10457496222113710703)
XLA Ops:
  14.4 13.0 %all-reduce = s32[8]{0:T(128)S(1)} all-reduce(s32[8]{0:T(128)S(1)} %dynamic-update-slice), channel_id=1, replica_groups=mesh['dom'=64,'cls'=8] {'cls'}, use_global_device_ids=true, to_apply=%add | all-reduce | flops 8 | bytes 64
  28.3 27.1 %all_gather.9 = bf16[8,8,2,1024]{3,1,2,0:T(8,128)(2,1)S(1)} all-gather(bf16[1,8,2,1024]{3,1,2,0:T(8,128)(2,1)S(1)} %reshape.517), channel_id=1, replica_groups=mesh['dom'=64,'cls'=8] {'cls'}, dimensions={0}, use_global_device_ids=true | all-gather | bytes 294912 | tf_op jit(solution)/shard_map/all_gather | solution.py:126
  57.7 87.6 %all-gather = f32[64,64,12]{1,2,0:T(8,128)S(1)} all-gather(f32[1,64,12]{1,2,0:T(8,128)S(1)} %bitcast.282), channel_id=1, replica_groups=mesh['dom'=64,'cls'=8] {'dom'}, dimensions={0}, use_global_device_ids=true | all-gather | bytes 199680 | tf_op jit(solution)/shard_map/all_gather | solution.py:129
  148.8 140.1 %while.14 = (s32[]{:T(128)}, f32[12,8]{1,0:T(8,128)S(1)}, f32[12,8]{1,0:T(8,128)S(1)}, f32[12,8,2,1024]{3,1,2,0:T(8,128)}, f32[8,8,2,1024]{3,1,0,2:T(8,128)}, /*...) while((s32[]{:T(128)}, f32[12,8]{1,0:T(8,128)S(1)}, ...), condition=%wide.region_6.7_spmd, body=%wide.region_1.6_spmd.sunk | while | flops 138674160 | bytes 8921689 | solution.py:141
  151.5 2.3 fusion.116
  154.5 2.2 convert_bitcast_fusion.2
  156.7 1.9 copy.111
  163.2 2.3 fusion.116
  166.1 2.2 convert_bitcast_fusion.2
  174.9 2.3 fusion.116
  177.8 2.2 convert_bitcast_fusion.2
  186.5 2.3 fusion.116
  189.5 2.2 convert_bitcast_fusion.2
  198.2 2.3 fusion.116
  201.2 2.2 convert_bitcast_fusion.2
  209.9 2.3 fusion.116
  212.8 2.2 convert_bitcast_fusion.2
  221.6 2.3 fusion.116
  224.5 2.2 convert_bitcast_fusion.2
  233.2 2.3 fusion.116
  236.2 2.2 convert_bitcast_fusion.2
  244.9 2.3 fusion.116
  247.8 2.2 convert_bitcast_fusion.2
  256.6 2.3 fusion.116
  259.5 2.2 convert_bitcast_fusion.2
  268.2 2.3 fusion.116
  271.2 2.2 convert_bitcast_fusion.2
  279.9 2.3 fusion.116
  282.9 2.2 convert_bitcast_fusion.2
  289.0 16.5 %pmax.7 = f32[8]{0:T(128)S(1)} all-reduce(f32[8]{0:T(128)S(1)} %reduce_max.18), channel_id=1, replica_groups=mesh['dom'=64,'cls'=8] {'cls'}, use_global_device_ids=true, to_apply=%region_8.9 | all-reduce | flops 8 | bytes 64 | tf_op jit(solution)/shard_map/pmax | solution.py:146
  305.5 17.3 %psum.7 = f32[8]{0:T(128)S(1)} all-reduce(f32[8]{0:T(128)S(1)} %multiply_reduce_fusion), channel_id=1, replica_groups=mesh['dom'=64,'cls'=8] {'cls'}, use_global_device_ids=true, to_apply=%region_10.11 | all-reduce | flops 8 | bytes 64 | tf_op jit(solution)/shard_map/psum | solution.py:147
  327.9 141.9 %reduce-scatter.4.cloned.1.call-done = f32[16,36]{1,0:T(8,128)} async-done(((f32[1024,36]{1,0:T(8,128)}), f32[16,36]{1,0:T(8,128)}) %reduce-scatter.4.cloned.1.call-update) | async-done | bytes 2320
  (260 shorter events, 103.2 us)
Async XLA Ops:
  7.2 49.2 %copy-start = (f32[16,23]{1,0:T(8,128)S(1)}, f32[16,23]{1,0:T(8,128)}, u32[]{:S(2)}) copy-start(f32[16,23]{1,0:T(8,128)} %param.10) | copy-start | bytes 4420
  7.2 462.6 %reduce-scatter.4.cloned.1.call-start = ((), (), s32[]{:S(2)}) async-start(), calls=%async_computation.1 | async-start | bytes 532480
  9.6 48.1 %copy-start.1 = (f32[12,64]{1,0:T(8,128)S(1)}, f32[12,64]{1,0:T(8,128)}, u32[]{:S(2)}) copy-start(f32[12,64]{1,0:T(8,128)} %param.9) | copy-start | bytes 9220
Sparse Core Ops, SparseCore 0:
  327.5 142.2 reduce-scatter.3
where the time goes:
time: 480 us; the launch traced here: 478 us
  blocking collectives  162 us (34%)
  waiting for transfers between devices  142 us (30%)
  local copies, waits for them, and re-layouts  73.4 us (15%)
  matrix products  60.1 us (13%)
  other arithmetic  25.5 us (5%)
  between operations  15 us (3%)
    unnamed x2, waiting for transfers between devices  142 us
    all_gather x1, blocking collectives, shards(): maps = lax.all_gather(references, 'dom', axis=1, tiled=True)  87.6 us
    dot_general x25, matrix products, product(): return jnp.einsum(form, left, right, preferred_element_type=jnp.float32)  54.3 us
    convert_element_type x24, local copies, waits for them, and re-layouts, class_step(): what = what.reshape(count, ROT, 2, BAND * BAND).astype(jnp.float32)  34.5 us
    all_gather x1, blocking collectives, shards(): lax.all_gather(own_bands, 'cls', axis=0, tiled=True)  27.1 us
    another operation x24, local copies, waits for them, and re-layouts, class_step(): jnp.stack([breal, bimag], axis=2).astype(jnp.bfloat16)  18.2 us
    psum x1, blocking collectives, shards(): lax.psum(jnp.sum(jnp.exp(peaks - top[None, :]) * totals, axis=0), 'cls')  17.3 us
    pmax x1, blocking collectives, shards(): top = lax.pmax(local_top, 'cls')  16.5 us
  transfers between devices with their start and end apart: 1, of which 1 were waited for; matrix products, arithmetic and copies ran while one was open for 0% of the time, Pallas kernels for 0%

commit v1 on v0

--- a/solution.py
+++ b/solution.py
@@ -126,7 +126,9 @@
         lax.all_gather(own_bands, "cls", axis=0, tiled=True),
         lax.all_gather(group_ids, "cls", axis=0, tiled=True),
     )
-    maps = lax.all_gather(references, "dom", axis=1, tiled=True)
+    maps = jnp.concatenate(
+        lax.all_to_all(jnp.stack([references] * lax.axis_size("dom")), "dom", 0, 0), axis=1
+    )
     complete_input = fourier_input.astype(jnp.float32)
     contrast_transfer, noise_deviation = spectra(ctf_profile, noise_power, block_labels)
     abstract_value = (

time: 480 us -> 418 us (0.87)
  the two profiles are of different devices: /device:TPU:4 before, /device:TPU:2 now
where the time goes in v1:
time: 418 us; the launch traced here: 416 us
  waiting for transfers between devices  149 us (36%)
  local copies, waits for them, and re-layouts  75.3 us (18%)
  blocking collectives  74 us (18%)
  matrix products  59.5 us (14%)
  other arithmetic  26.7 us (6%)
  starting transfers between devices  16.6 us (4%)
  between operations  15 us (4%)
    unnamed x2, waiting for transfers between devices  149 us
    dot_general x25, matrix products, product(): return jnp.einsum(form, left, right, preferred_element_type=jnp.float32)  54.3 us
    convert_element_type x24, local copies, waits for them, and re-layouts, class_step(): what = what.reshape(count, ROT, 2, BAND * BAND).astype(jnp.float32)  34.5 us
    all_gather x1, blocking collectives, shards(): lax.all_gather(own_bands, 'cls', axis=0, tiled=True)  26.9 us
    pmax x1, blocking collectives, shards(): top = lax.pmax(local_top, 'cls')  18.8 us
    another operation x24, local copies, waits for them, and re-layouts, class_step(): jnp.stack([breal, bimag], axis=2).astype(jnp.bfloat16)  18.2 us
    psum x1, blocking collectives, shards(): lax.psum(jnp.sum(jnp.exp(peaks - top[None, :]) * totals, axis=0), 'cls')  17.2 us
    all_to_all x1, starting transfers between devices, shards(): lax.all_to_all(jnp.stack([references] * lax.axis_size('dom')), 'dom', 0, 0)  16.6 us
  transfers between devices with their start and end apart: 2, of which 1 were waited for; matrix products, arithmetic and copies ran while one was open for 2% of the time, Pallas kernels for 0%

profile of v1, /device:TPU:2, one launch (start us, length us, event | category | flops | bytes accessed | tf_op | source)
XLA Modules:
  0.0 416.4 jit_solution(5911592804548870460)
XLA Ops:
  8.9 16.6 %all-to-all-start = ((f32[64,1,768]{2,1,0:T(1,128)}), f32[64,1,768]{2,1,0:T(1,128)S(1)}, u32[]{:S(2)}, u32[]{:S(2)}) async-start(f32[64,1,768]{2,1,0:T(1,128)} %reshape.555), calls=%async_computation | async-start | bytes 393216 | tf_op jit(solution)/shard_map/all_to_all | solution.py:130
  32.6 11.0 %all-reduce = s32[8]{0:T(128)S(1)} all-reduce(s32[8]{0:T(128)S(1)} %dynamic-update-slice), channel_id=1, replica_groups=mesh['dom'=64,'cls'=8] {'cls'}, use_global_device_ids=true, to_apply=%add | all-reduce | flops 8 | bytes 64
  44.6 26.9 %all_gather.6 = bf16[8,8,2,1024]{3,1,2,0:T(8,128)(2,1)S(1)} all-gather(bf16[1,8,2,1024]{3,1,2,0:T(8,128)(2,1)S(1)} %reshape.519), channel_id=1, replica_groups=mesh['dom'=64,'cls'=8] {'cls'}, dimensions={0}, use_global_device_ids=true | all-gather | bytes 294912 | tf_op jit(solution)/shard_map/all_gather | solution.py:126
  78.0 140.2 %while.14 = (s32[]{:T(128)}, f32[12,8]{1,0:T(8,128)S(1)}, f32[12,8]{1,0:T(8,128)S(1)}, f32[12,8,2,1024]{3,1,2,0:T(8,128)}, f32[8,8,2,1024]{3,1,0,2:T(8,128)}, /*...) while((s32[]{:T(128)}, f32[12,8]{1,0:T(8,128)S(1)}, ...), condition=%wide.region_6.7_spmd, body=%wide.region_1.6_spmd.sunk | while | flops 138674160 | bytes 8921689 | solution.py:143
  80.6 2.3 fusion.117
  83.6 2.2 convert_bitcast_fusion.2
  85.8 1.9 copy.129
  92.3 2.3 fusion.117
  95.3 2.2 convert_bitcast_fusion.2
  104.0 2.3 fusion.117
  107.0 2.2 convert_bitcast_fusion.2
  115.7 2.3 fusion.117
  118.6 2.2 convert_bitcast_fusion.2
  127.4 2.3 fusion.117
  130.3 2.2 convert_bitcast_fusion.2
  139.1 2.3 fusion.117
  142.0 2.2 convert_bitcast_fusion.2
  150.7 2.3 fusion.117
  153.7 2.2 convert_bitcast_fusion.2
  162.4 2.3 fusion.117
  165.4 2.2 convert_bitcast_fusion.2
  174.1 2.3 fusion.117
  177.0 2.2 convert_bitcast_fusion.2
  185.8 2.3 fusion.117
  188.7 2.2 convert_bitcast_fusion.2
  197.5 2.3 fusion.117
  200.4 2.2 convert_bitcast_fusion.2
  209.1 2.3 fusion.117
  212.1 2.2 convert_bitcast_fusion.2
  218.2 18.8 %pmax.7 = f32[8]{0:T(128)S(1)} all-reduce(f32[8]{0:T(128)S(1)} %reduce_max.18), channel_id=1, replica_groups=mesh['dom'=64,'cls'=8] {'cls'}, use_global_device_ids=true, to_apply=%region_8.9 | all-reduce | flops 8 | bytes 64 | tf_op jit(solution)/shard_map/pmax | solution.py:148
  237.1 17.2 %psum.7 = f32[8]{0:T(128)S(1)} all-reduce(f32[8]{0:T(128)S(1)} %multiply_reduce_fusion), channel_id=1, replica_groups=mesh['dom'=64,'cls'=8] {'cls'}, use_global_device_ids=true, to_apply=%region_10.11 | all-reduce | flops 8 | bytes 64 | tf_op jit(solution)/shard_map/psum | solution.py:149
  259.4 148.5 %reduce-scatter.4.cloned.1.call-done = f32[16,36]{1,0:T(8,128)} async-done(((f32[1024,36]{1,0:T(8,128)}), f32[16,36]{1,0:T(8,128)}) %reduce-scatter.4.cloned.1.call-update) | async-done | bytes 2320
  (263 shorter events, 105.7 us)
Async XLA Ops:
  7.2 64.6 %copy-start = (f32[16,23]{1,0:T(8,128)S(1)}, f32[16,23]{1,0:T(8,128)}, u32[]{:S(2)}) copy-start(f32[16,23]{1,0:T(8,128)} %param.10) | copy-start | bytes 4420
  7.2 64.4 %copy-start.1 = (f32[23]{0:T(128)S(1)}, f32[23]{0:T(128)}, u32[]{:S(2)}) copy-start(f32[23]{0:T(128)} %param.11) | copy-start | bytes 280
  8.9 64.4 %all-to-all-start = ((f32[64,1,768]{2,1,0:T(1,128)}), f32[64,1,768]{2,1,0:T(1,128)S(1)}, u32[]{:S(2)}, u32[]{:S(2)}) async-start(f32[64,1,768]{2,1,0:T(1,128)} %reshape.555), calls=%async_computation | async-start | bytes 393216 | tf_op jit(solution)/shard_map/all_to_all | solution.py:130
  25.5 382.5 %reduce-scatter.4.cloned.1.call-start = ((), (), s32[]{:S(2)}) async-start(), calls=%async_computation.2 | async-start | bytes 532480
Sparse Core Ops, SparseCore 0:
  259.0 148.8 reduce-scatter.3
